TPU v7x, 256 devices: a whole 4x4x8 slice. The times are simulated.
256 devices in a mesh: dp: 16 (over x, y_hi, core), seq: 16 (over z, y_lo).
Axes of the slice: x: 4, y: 4 (y_hi: 2, y_lo: 2; y = y_hi * 2 + y_lo), z: 8, core: 2. Of those that a mesh axis runs over, the one named last changes fastest.
Arguments:
- queries: bfloat16 [40960, 768], P(('dp', 'seq')), may hold values from -8 to 8
- keys: bfloat16 [40960, 768], P(('dp', 'seq')), may hold values from -8 to 8
- values: bfloat16 [40960, 768], P(('dp', 'seq')), may hold values from -6 to 6
- frames: bfloat16 [40960, 768], P(('dp', 'seq')), may hold values from -4 to 4
- upstream: bfloat16 [40960, 768], P(('dp', 'seq')), may hold values from -6 to 6
- lengths: int32 [16], P('dp'), may hold values from 640 to 2560, as said below
- conv_kernel: bfloat16 [32, 768], replicated, may hold values from -1 to 1
Outputs:
- out: bfloat16 [40960, 768], P(('dp', 'seq'))
- query_grad: bfloat16 [40960, 768], P(('dp', 'seq'))
- key_grad: bfloat16 [40960, 768], P(('dp', 'seq'))
- value_grad: bfloat16 [40960, 768], P(('dp', 'seq'))
- frame_grad: bfloat16 [40960, 768], P(('dp', 'seq'))
- kernel_grad: float32 [32, 768], replicated
Inputs may be any that keep to these rules, and one draw needn't show every extreme that they name: `lengths`: one utterance has all 2560 frames live and another has 640.
All inputs are finite; a program needn't handle non-finite values.
Results may differ from a plain program's by a relative error of at most 0.0262.
Values may be sent and summed in bfloat16 or wider, within the bound.
No kernel may reach another device: no remote copies, remote signals or barrier semaphores. Data moves between devices by JAX's collectives and lax.ppermute only.
A program may use at most 128 MiB of HBM per device.

v0:
```python
import jax
import jax.numpy as jnp
from jax import lax
from jax.sharding import PartitionSpec as P

HEAD_DIM = 64
KERNEL = 32


def shifted(x, axis, by):
    count = lax.axis_size(axis)
    pairs = [(i, i + by) for i in range(count) if 0 <= i + by < count]
    return lax.ppermute(x, axis, pairs)


def per_device(queries, keys, values, frames, upstream, lengths, conv_kernel):
    row_count = queries.shape[0]
    channels = queries.shape[1]
    head_count = channels // HEAD_DIM
    seq_count = lax.axis_size("seq")
    first_row = lax.axis_index("seq") * row_count
    length = lengths[0]
    score_scale = HEAD_DIM ** (-0.5)
    span = row_count * seq_count
    shards = 1
    while shards * row_count < 512 and seq_count % (2 * shards) == 0:
        shards = shards * 2
    key_block = row_count * shards
    block_count = span // key_block
    key_all, value_all = (
        lax.all_gather(keys, "seq", axis=0, tiled=True),
        lax.all_gather(values, "seq", axis=0, tiled=True),
    )
    key_blocks = key_all.reshape(block_count, key_block, head_count, HEAD_DIM)
    value_blocks = value_all.reshape(block_count, key_block, head_count, HEAD_DIM)
    block_starts = jnp.arange(block_count, dtype=jnp.int32) * key_block
    query_heads = queries.reshape(row_count, head_count, HEAD_DIM)

    def block_scores(key_part, block_start):
        scores = (
            jnp.einsum("thd,khd->htk", query_heads, key_part, preferred_element_type=jnp.float32)
            * score_scale
        )
        key_live = block_start + jnp.arange(key_part.shape[0], dtype=jnp.int32) < length
        return jnp.where(key_live[None, None, :], scores, -jnp.inf)

    def running_total(state_pair, block_items):
        running_top, total_sum = state_pair
        key_part, block_start = block_items
        scores = block_scores(key_part, block_start)
        higher = jnp.maximum(running_top, jnp.max(scores, axis=2))
        total_sum = total_sum * jnp.exp(running_top - higher) + jnp.sum(
            jnp.exp(scores - higher[:, :, None]), axis=2
        )
        return ((higher, total_sum), None)

    start_state = (
        jnp.full((head_count, row_count), -1e30, jnp.float32),
        jnp.zeros((head_count, row_count), jnp.float32),
    )
    (running_top, total_sum), unused = lax.scan(
        running_total, start_state, (key_blocks, block_starts)
    )
    log_total = running_top + jnp.log(total_sum)

    def attend_block(attend_acc, block_items):
        key_part, value_part, block_start = block_items
        prob_bf = jnp.exp(block_scores(key_part, block_start) - log_total[:, :, None]).astype(
            jnp.bfloat16
        )
        return (
            attend_acc
            + jnp.einsum("htk,khd->thd", prob_bf, value_part, preferred_element_type=jnp.float32),
            None,
        )

    attend_acc, unused = lax.scan(
        attend_block,
        jnp.zeros((row_count, head_count, HEAD_DIM), jnp.float32),
        (key_blocks, value_blocks, block_starts),
    )
    attended = attend_acc.reshape(row_count, channels).astype(jnp.bfloat16)
    frame_live = (first_row + jnp.arange(row_count, dtype=jnp.int32) < length)[:, None]
    hidden = (frames.astype(jnp.float32) + attended.astype(jnp.float32)).astype(jnp.bfloat16)
    masked = jnp.where(frame_live, hidden, jnp.zeros_like(hidden))
    past_rows = shifted(masked[row_count - (KERNEL - 1) :], "seq", 1)
    extended = jnp.concatenate([past_rows, masked], axis=0).astype(jnp.float32)
    weights = conv_kernel.astype(jnp.float32)
    conv_out = jnp.zeros((row_count, channels), jnp.float32)
    for tap_index in range(KERNEL):
        conv_out = (
            conv_out
            + weights[tap_index]
            * extended[KERNEL - 1 - tap_index : KERNEL - 1 - tap_index + row_count]
        )
    sig_conv = jax.nn.sigmoid(conv_out)
    out = (hidden.astype(jnp.float32) + conv_out * sig_conv).astype(jnp.bfloat16)
    loss_grad = jnp.where(frame_live, upstream.astype(jnp.float32), 0.0)
    conv_grad = (loss_grad * sig_conv * (1.0 + conv_out * (1.0 - sig_conv))).astype(jnp.bfloat16)
    conv_float = conv_grad.astype(jnp.float32)
    kernel_part = jnp.stack(
        [
            jnp.sum(
                conv_float * extended[KERNEL - 1 - tap_index : KERNEL - 1 - tap_index + row_count],
                axis=0,
            )
            for tap_index in range(KERNEL)
        ]
    )
    future_rows = shifted(conv_grad[: KERNEL - 1], "seq", -1)
    ahead_rows = jnp.concatenate([conv_grad, future_rows], axis=0).astype(jnp.float32)
    back_conv = jnp.zeros((row_count, channels), jnp.float32)
    for tap_index in range(KERNEL):
        back_conv = back_conv + weights[tap_index] * ahead_rows[tap_index : tap_index + row_count]
    frame_grad = (loss_grad + jnp.where(frame_live, back_conv, 0.0)).astype(jnp.bfloat16)
    grad_heads = frame_grad.reshape(row_count, head_count, HEAD_DIM)
    attended_heads = attended.reshape(row_count, head_count, HEAD_DIM)
    delta_rows = jnp.sum(
        grad_heads.astype(jnp.float32) * attended_heads.astype(jnp.float32), axis=2
    ).T

    def score_grads(key_part, value_part, block_start):
        soft_weights = jnp.exp(block_scores(key_part, block_start) - log_total[:, :, None])
        prob_grad = jnp.einsum(
            "thd,khd->htk", grad_heads, value_part, preferred_element_type=jnp.float32
        )
        score_grad = (soft_weights * (prob_grad - delta_rows[:, :, None])).astype(jnp.bfloat16)
        return (soft_weights.astype(jnp.bfloat16), score_grad)

    def gradient_block(query_acc, block_items):
        key_part, value_part, block_start = block_items
        prob_bf, score_grad = score_grads(key_part, value_part, block_start)
        query_acc = query_acc + jnp.einsum(
            "htk,khd->thd", score_grad, key_part, preferred_element_type=jnp.float32
        )
        key_term = (
            jnp.einsum("htk,thd->khd", score_grad, query_heads, preferred_element_type=jnp.float32)
            * score_scale
        )
        value_term = jnp.einsum(
            "htk,thd->khd", prob_bf, grad_heads, preferred_element_type=jnp.float32
        )
        grad_terms = jnp.concatenate(
            [key_term.reshape(key_block, channels), value_term.reshape(key_block, channels)], axis=1
        )
        return (query_acc, grad_terms)

    query_acc, grad_terms = lax.scan(
        gradient_block,
        jnp.zeros((row_count, head_count, HEAD_DIM), jnp.float32),
        (key_blocks, value_blocks, block_starts),
    )
    own_rows = lax.psum_scatter(
        grad_terms.reshape(span, 2 * channels).astype(jnp.bfloat16),
        "seq",
        scatter_dimension=0,
        tiled=True,
    ).astype(jnp.float32)
    key_grad = own_rows[:, :channels].astype(jnp.bfloat16)
    value_grad = own_rows[:, channels:].astype(jnp.bfloat16)
    query_grad = (query_acc * score_scale).reshape(row_count, channels).astype(jnp.bfloat16)
    kernel_total = lax.psum(kernel_part, ("dp", "seq"))
    kernel_grad = kernel_total / lax.axis_size("dp")
    return (out, query_grad, key_grad, value_grad, frame_grad, kernel_grad)


def solution(mesh):
    placed = (
        P(("dp", "seq"), None),
        P(("dp", "seq"), None),
        P(("dp", "seq"), None),
        P(("dp", "seq"), None),
        P(("dp", "seq"), None),
        P("dp"),
        P(),
    )
    return jax.shard_map(
        per_device,
        mesh=mesh,
        in_specs=placed,
        out_specs=(
            P(("dp", "seq"), None),
            P(("dp", "seq"), None),
            P(("dp", "seq"), None),
            P(("dp", "seq"), None),
            P(("dp", "seq"), None),
            P(),
        ),
        check_vma=False,
    )
```

profile of v0, /device:TPU:1, one launch (start us, length us, event | category | flops | bytes accessed | tf_op | source)
XLA Modules:
  0.0 772.7 jit_solution(14482289051030039429)
XLA Ops:
  13.8 92.2 %all-gather.5.cloned.1.call-done = bf16[2560,768]{1,0:T(8,128)(2,1)} async-done(((bf16[160,768]{1,0:T(8,128)(2,1)}), bf16[2560,768]{1,0:T(8,128)(2,1)}) %all-gather.5.cloned.1.call-update) | async-done | bytes 3932176 | tf_op jit(solution)/shard_map/all_gather | solution.py:31
  106.1 6.2 copy.23
  112.3 7.6 reshape.64
  119.9 82.5 %all-gather.3.cloned.1.call-done = bf16[2560,768]{1,0:T(8,128)(2,1)} async-done(((bf16[160,768]{1,0:T(8,128)(2,1)}), bf16[2560,768]{1,0:T(8,128)(2,1)}) %all-gather.3.cloned.1.call-update) | async-done | bytes 3932176 | tf_op jit(solution)/shard_map/all_gather | solution.py:32
  202.4 6.2 copy.22
  208.6 7.6 reshape.63
  216.2 5.0 copy.26
  221.2 2.7 copy.25
  223.9 22.7 %while.37 = (s32[]{:T(128)}, f32[12,160]{1,0:T(8,128)S(1)}, f32[12,160]{1,0:T(8,128)S(1)}, s32[4]{0:T(128)S(1)}, s32[]{:T(128)}, /*index=5*/bf16[4,640,12,64]{1,...) while((s32[]{:T(128)}, f32[12,160]{1,0:T(8,128)S(1)}, ...), condition=%wide.region_3.4_spmd.clone, body=%wide.region_0.3_spmd.clone.sunk | while | flops 165898880 | bytes 11161096 | solution.py:61
  224.5 1.3 add_compare_fusion.7
  225.8 2.2 bitcast_reduce_fusion.2
  228.0 1.5 fusion.145
  230.2 1.3 add_compare_fusion.7
  231.5 2.2 bitcast_reduce_fusion.2
  233.7 1.5 fusion.145
  235.9 1.3 add_compare_fusion.7
  237.2 2.2 bitcast_reduce_fusion.2
  239.4 1.5 fusion.145
  241.5 1.3 add_compare_fusion.7
  242.8 2.2 bitcast_reduce_fusion.2
  245.0 1.5 fusion.145
  246.6 43.0 %while.38 = (s32[]{:T(128)}, f32[160,12,64]{0,2,1:T(8,128)}, bf16[4,640,12,64]{1,3,2,0:T(8,128)(2,1)}, s32[4]{0:T(128)S(1)}, s32[]{:T(128)}, /*index=5*/bf16[4,6...) while((s32[]{:T(128)}, f32[160,12,64]{0,2,1:T(8,128)}, ...), condition=%wide.region_5.6_spmd.clone, body=%wide.region_4.5_spmd.clone.sunk | while | flops 319735040 | bytes 5464979 | solution.py:77
  248.5 4.5 constant_dynamic-slice_fusion.2
  253.0 4.2 fusion.150
  259.1 4.5 constant_dynamic-slice_fusion.2
  263.6 4.4 fusion.150
  269.9 4.5 constant_dynamic-slice_fusion.2
  274.4 4.4 fusion.150
  279.4 1.3 add_compare_fusion.8
  280.7 4.5 constant_dynamic-slice_fusion.2
  285.2 4.4 fusion.150
  291.1 2.7 collective-permute-start
  293.8 1.9 slice_reduce_fusion.30
  297.1 14.6 %fusion.79 = (f32[768]{0:T(1024)S(1)}, f32[768]{0:T(1024)S(1)}, f32[768]{0:T(1024)S(1)}, f32[768]{0:T(1024)S(1)}, f32[768]{0:T(1024)S(1)}, /*index=5*/f32[768]{0...) fusion(f32[191,768]{0,1:T(8,128)S(1)} %maximum_convert_fusion, ...), kind=kLoop, calls=%fused_computation.121 | loop fusion | flops 13625856 | bytes 16865440 | tf_op jit(solution)/shard_map/reduce_sum | solution.py:103
  312.9 4.7 fusion.78
  336.5 5.4 stack.131
  342.4 13.5 %fusion.83 = bf16[160,768]{0,1:T(8,128)(2,1)S(1)} fusion(f32[191,768]{0,1:T(8,128)S(1)} %maximum_convert_fusion.1, bf16[160,768]{0,1:T(8,128)(2,1)S(1)} %copy.29, f32[768]{0:T(1024)S(1)} %get-tuple-element.320, f32[768]{0:T(1024)S(1)} %get-tuple-element.321, f32[768]{0:T(1024)S(1)} %get-tuple-element.322, f32[768]{0:T(1024)} %get-tuple-element.323, ...), kind=kLoop, calls=%fused_computation.126 | loop fusion | flops 8355840 | bytes 16318624 | tf_op jit(solution)/shard_map/convert_element_type | solution.py:115
  356.1 50.8 %while.39 = (s32[]{:T(128)}, f32[160,12,64]{0,2,1:T(8,128)S(1)}, bf16[4,640,1536]{1,2,0:T(8,128)(2,1)}, bf16[4,640,12,64]{1,3,2,0:T(8,128)(2,1)}, s32[4]{0:T(128...) while((s32[]{:T(128)}, f32[160,12,64]{0,2,1:T(8,128)S(1)}, ...), condition=%wide.region_8.9_spmd.clone, body=%wide.region_7.8_spmd.clone.sunk | while | flops 803882240 | bytes 32956980 | solution.py:148
  358.0 2.1 fusion.161
  360.1 1.4 fusion.163
  361.4 3.0 multiply_convert_fusion.5
  364.4 2.4 fusion.162
  367.4 1.5 fusion.164
  370.7 2.1 fusion.161
  372.8 1.4 fusion.163
  374.1 3.0 multiply_convert_fusion.5
  377.1 2.4 fusion.162
  380.1 1.5 fusion.164
  383.4 2.1 fusion.161
  385.5 1.4 fusion.163
  386.8 3.0 multiply_convert_fusion.5
  389.8 2.4 fusion.162
  392.8 1.5 fusion.164
  394.8 1.3 add_compare_fusion.9
  396.1 2.1 fusion.161
  398.2 1.4 fusion.163
  399.5 3.0 multiply_convert_fusion.5
  402.5 2.4 fusion.162
  405.5 1.5 fusion.164
  406.9 10.7 %copy.32 = bf16[4,640,1536]{2,1,0:T(8,128)(2,1)} copy(bf16[4,640,1536]{1,2,0:T(8,128)(2,1)} %get-tuple-element.148) | data formatting | bytes 15728640 | tf_op jit(solution)/shard_map/convert_element_type | solution.py:154
  421.6 172.5 %all-reduce.2.cloned.1.call-done = f32[32,768]{1,0:T(8,128)} async-done(((f32[32,768]{1,0:T(8,128)}), f32[32,768]{1,0:T(8,128)}) %all-reduce.2.cloned.1.call-update) | async-done | bytes 98320 | tf_op jit(solution)/shard_map/psum | solution.py:162
  594.1 1.5 broadcast_multiply_fusion
  595.6 168.7 %reduce-scatter.2.cloned.1.call-done = bf16[160,1536]{1,0:T(8,128)(2,1)} async-done(((bf16[2560,1536]{1,0:T(8,128)(2,1)}), bf16[160,1536]{1,0:T(8,128)(2,1)}) %reduce-scatter.2.cloned.1.call-update) | async-done | bytes 491536 | tf_op jit(solution)/shard_map/reduce_scatter | solution.py:153
  764.3 1.9 fusion.115
  (121 shorter events, 50.5 us)
Async XLA Ops:
  7.2 98.9 %all-gather.5.cloned.1.call-start = ((), (), s32[]{:S(2)}) async-start(), calls=%async_computation.2 | async-start | bytes 4177920 | tf_op jit(solution)/shard_map/all_gather | solution.py:31
  7.9 194.5 %all-gather.3.cloned.1.call-start = ((), (), s32[]{:S(2)}) async-start(), calls=%async_computation.1 | async-start | bytes 4177920 | tf_op jit(solution)/shard_map/all_gather | solution.py:32
  8.6 585.4 %all-reduce.2.cloned.1.call-start = ((), (), s32[]{:S(2)}) async-start(), calls=%async_computation.4 | async-start | bytes 196608 | tf_op jit(solution)/shard_map/psum | solution.py:162
  10.2 102.1 %copy-start.3 = (f32[32,768]{1,0:T(8,128)}, f32[32,768]{1,0:T(8,128)S(1)}, u32[]{:S(2)}) copy-start(f32[32,768]{1,0:T(8,128)S(1)} %convert_element_type.78) | copy-start | bytes 294916
  13.1 277.8 %copy-start.6 = (pred[160]{0:T(512)(128)(4,1)}, pred[160]{0:T(512)(128)(4,1)S(1)}, u32[]{:S(2)}) copy-start(pred[160]{0:T(512)(128)(4,1)S(1)} %add_compare_fusion.3) | copy-start | bytes 484
  216.2 5.0 copy-start
  289.6 6.1 copy-start.4
  289.6 6.1 copy-start.7
  291.1 5.8 collective-permute-start
  311.6 30.6 %collective-permute-start.1 = (bf16[31,768]{0,1:T(8,128)(2,1)S(1)}, bf16[31,768]{0,1:T(8,128)(2,1)S(1)}, u32[]{:S(2)}, u32[]{:S(2)}) collective-permute-start(bf16[31,768]{0,1:T(8,128)(2,1)S(1)} %slice.531), channel_id=1, source_target_pairs={{1,0},{2,1},{3,2},{4,3},{5,4},{6,5},{7,6},{8,7},{9,8},{10,9},{11,1... | collective-permute-start | bytes 142856 | tf_op jit(solution)/shard_map/ppermute | solution.py:13
  342.0 422.3 %reduce-scatter.2.cloned.1.call-start = ((), (), s32[]{:S(2)}) async-start(), calls=%async_computation.3 | async-start | bytes 8355840 | tf_op jit(solution)/shard_map/reduce_scatter | solution.py:153
  342.4 13.5 %copy-start.2 = (f32[160,12,64]{0,2,1:T(8,128)S(1)}, f32[160,12,64]{0,2,1:T(8,128)}, u32[]{:S(2)}) copy-start(f32[160,12,64]{0,2,1:T(8,128)} %get-tuple-element.146) | copy-start | bytes 1474564
  342.4 13.7 %copy-start.5 = (f32[12,160]{1,0:T(8,128)S(1)}, f32[12,160]{1,0:T(8,128)}, u32[]{:S(2)}) copy-start(f32[12,160]{1,0:T(8,128)} %copy-done.4) | copy-start | bytes 23044
  342.4 13.7 %copy-start.8 = (s32[4]{0:T(128)S(1)}, s32[4]{0:T(128)}, u32[]{:S(2)}) copy-start(s32[4]{0:T(128)} %copy-done.7) | copy-start | bytes 52
  417.6 1.1 copy-start.1
Sparse Core Ops, SparseCore 0:
  9.8 96.2 all-gather.4
  107.8 94.5 all-gather.2
  342.1 251.9 all-reduce.1
  596.5 167.7 reduce-scatter.1
where the time goes:
time: 775 us; the launch traced here: 773 us
  waiting for transfers between devices  517 us (67%)
  local copies, waits for them, and re-layouts  108 us (14%)
  other arithmetic  64.8 us (8%)
  matrix products  63.5 us (8%)
  between operations  14.7 us (2%)
    psum x1, waiting for transfers between devices, per_device(): kernel_total = lax.psum(kernel_part, ('dp', 'seq'))  173 us
    reduce_scatter x1, waiting for transfers between devices, per_device(): lax.psum_scatter(grad_terms.reshape(span, 2 * channels).astype(jnp.bfloat...  169 us
    all_gather x1, waiting for transfers between devices, per_device(): lax.all_gather(keys, 'seq', axis=0, tiled=True)  92.2 us
    all_gather x1, waiting for transfers between devices, per_device(): lax.all_gather(values, 'seq', axis=0, tiled=True)  82.5 us
    dynamic_slice x16, local copies, waits for them, and re-layouts, per_device(): lax.scan(running_total, start_state, (key_blocks, block_starts))  24.9 us
    another operation x33, local copies, waits for them, and re-layouts, per_device(): jnp.stack([jnp.sum(conv_float * extended[KERNEL - 1 - tap_index:KERNEL -...  24.3 us
    reduce_sum x2, other arithmetic, per_device(): jnp.sum(conv_float * extended[KERNEL - 1 - tap_index:KERNEL - 1 - tap_ind...  19.2 us
    dot_general x4, matrix products, attend_block(): jnp.einsum('htk,khd->thd', prob_bf, value_part, preferred_element_type=jn...  17.5 us
  transfers between devices with their start and end apart: 6, of which 4 were waited for; matrix products, arithmetic and copies ran while one was open for 17% of the time, Pallas kernels for 0%

commit v1 on v0

--- a/solution.py
+++ b/solution.py
@@ -1,10 +1,12 @@
 import jax
 import jax.numpy as jnp
 from jax import lax
+from jax.sharding import Mesh
 from jax.sharding import PartitionSpec as P
 
 HEAD_DIM = 64
 KERNEL = 32
+GROUPS = 4
 
 
 def shifted(x, axis, by):
@@ -13,28 +15,50 @@
     return lax.ppermute(x, axis, pairs)
 
 
+def butterfly_sum(x, axes):
+    for axis in axes:
+        count = lax.axis_size(axis)
+        step = 1
+        while step < count:
+            x = x + lax.ppermute(x, axis, [(i, i ^ step) for i in range(count)])
+            step = step * 2
+    return x
+
+
 def per_device(queries, keys, values, frames, upstream, lengths, conv_kernel):
-    row_count = queries.shape[0]
+    rows = queries.shape[0]
     channels = queries.shape[1]
-    head_count = channels // HEAD_DIM
-    seq_count = lax.axis_size("seq")
-    first_row = lax.axis_index("seq") * row_count
+    sub_count = lax.axis_size("sb")
+    block_count_a = lax.axis_size("sa")
+    group = channels // sub_count
+    head_count = group // HEAD_DIM
+    row_count = rows * sub_count
+    span = row_count * block_count_a
+    block_index = lax.axis_index("sa")
+    group_index = lax.axis_index("sb")
+    first_row = block_index * row_count
     length = lengths[0]
     score_scale = HEAD_DIM ** (-0.5)
-    span = row_count * seq_count
-    shards = 1
-    while shards * row_count < 512 and seq_count % (2 * shards) == 0:
-        shards = shards * 2
-    key_block = row_count * shards
+
+    stacked = jnp.stack([queries, keys, values, frames, upstream])
+    mixed = lax.all_to_all(
+        stacked.reshape(5, rows, sub_count, group), "sb", 2, 1, tiled=True
+    ).reshape(5, row_count, group)
+    queries_b = mixed[0]
+    frames_b = mixed[3]
+    upstream_b = mixed[4]
+    kv_all = lax.all_gather(
+        jnp.concatenate([mixed[1], mixed[2]], axis=1), "sa", axis=0, tiled=True
+    )
+    key_all = kv_all[:, :group]
+    value_all = kv_all[:, group:]
+
+    key_block = row_count
     block_count = span // key_block
-    key_all, value_all = (
-        lax.all_gather(keys, "seq", axis=0, tiled=True),
-        lax.all_gather(values, "seq", axis=0, tiled=True),
-    )
     key_blocks = key_all.reshape(block_count, key_block, head_count, HEAD_DIM)
     value_blocks = value_all.reshape(block_count, key_block, head_count, HEAD_DIM)
     block_starts = jnp.arange(block_count, dtype=jnp.int32) * key_block
-    query_heads = queries.reshape(row_count, head_count, HEAD_DIM)
+    query_heads = queries_b.reshape(row_count, head_count, HEAD_DIM)
 
     def block_scores(key_part, block_start):
         scores = (
@@ -79,14 +103,16 @@
         jnp.zeros((row_count, head_count, HEAD_DIM), jnp.float32),
         (key_blocks, value_blocks, block_starts),
     )
-    attended = attend_acc.reshape(row_count, channels).astype(jnp.bfloat16)
+    attended = attend_acc.reshape(row_count, group).astype(jnp.bfloat16)
     frame_live = (first_row + jnp.arange(row_count, dtype=jnp.int32) < length)[:, None]
-    hidden = (frames.astype(jnp.float32) + attended.astype(jnp.float32)).astype(jnp.bfloat16)
+    hidden = (frames_b.astype(jnp.float32) + attended.astype(jnp.float32)).astype(jnp.bfloat16)
     masked = jnp.where(frame_live, hidden, jnp.zeros_like(hidden))
-    past_rows = shifted(masked[row_count - (KERNEL - 1) :], "seq", 1)
+    past_rows = shifted(masked[row_count - (KERNEL - 1) :], "sa", 1)
     extended = jnp.concatenate([past_rows, masked], axis=0).astype(jnp.float32)
-    weights = conv_kernel.astype(jnp.float32)
-    conv_out = jnp.zeros((row_count, channels), jnp.float32)
+    weights = lax.dynamic_slice_in_dim(conv_kernel, group_index * group, group, axis=1).astype(
+        jnp.float32
+    )
+    conv_out = jnp.zeros((row_count, group), jnp.float32)
     for tap_index in range(KERNEL):
         conv_out = (
             conv_out
@@ -95,7 +121,7 @@
         )
     sig_conv = jax.nn.sigmoid(conv_out)
     out = (hidden.astype(jnp.float32) + conv_out * sig_conv).astype(jnp.bfloat16)
-    loss_grad = jnp.where(frame_live, upstream.astype(jnp.float32), 0.0)
+    loss_grad = jnp.where(frame_live, upstream_b.astype(jnp.float32), 0.0)
     conv_grad = (loss_grad * sig_conv * (1.0 + conv_out * (1.0 - sig_conv))).astype(jnp.bfloat16)
     conv_float = conv_grad.astype(jnp.float32)
     kernel_part = jnp.stack(
@@ -107,9 +133,9 @@
             for tap_index in range(KERNEL)
         ]
     )
-    future_rows = shifted(conv_grad[: KERNEL - 1], "seq", -1)
+    future_rows = shifted(conv_grad[: KERNEL - 1], "sa", -1)
     ahead_rows = jnp.concatenate([conv_grad, future_rows], axis=0).astype(jnp.float32)
-    back_conv = jnp.zeros((row_count, channels), jnp.float32)
+    back_conv = jnp.zeros((row_count, group), jnp.float32)
     for tap_index in range(KERNEL):
         back_conv = back_conv + weights[tap_index] * ahead_rows[tap_index : tap_index + row_count]
     frame_grad = (loss_grad + jnp.where(frame_live, back_conv, 0.0)).astype(jnp.bfloat16)
@@ -141,7 +167,7 @@
             "htk,thd->khd", prob_bf, grad_heads, preferred_element_type=jnp.float32
         )
         grad_terms = jnp.concatenate(
-            [key_term.reshape(key_block, channels), value_term.reshape(key_block, channels)], axis=1
+            [key_term.reshape(key_block, group), value_term.reshape(key_block, group)], axis=1
         )
         return (query_acc, grad_terms)
 
@@ -151,40 +177,38 @@
         (key_blocks, value_blocks, block_starts),
     )
     own_rows = lax.psum_scatter(
-        grad_terms.reshape(span, 2 * channels).astype(jnp.bfloat16),
-        "seq",
+        grad_terms.reshape(span, 2 * group).astype(jnp.bfloat16),
+        "sa",
         scatter_dimension=0,
         tiled=True,
     ).astype(jnp.float32)
-    key_grad = own_rows[:, :channels].astype(jnp.bfloat16)
-    value_grad = own_rows[:, channels:].astype(jnp.bfloat16)
-    query_grad = (query_acc * score_scale).reshape(row_count, channels).astype(jnp.bfloat16)
-    kernel_total = lax.psum(kernel_part, ("dp", "seq"))
+    key_grad = own_rows[:, :group].astype(jnp.bfloat16)
+    value_grad = own_rows[:, group:].astype(jnp.bfloat16)
+    query_grad = (query_acc * score_scale).reshape(row_count, group).astype(jnp.bfloat16)
+    kernel_full = lax.dynamic_update_slice_in_dim(
+        jnp.zeros((KERNEL, channels), jnp.float32), kernel_part, group_index * group, axis=1
+    )
+    kernel_total = butterfly_sum(kernel_full, ("sb", "sa", "dp"))
     kernel_grad = kernel_total / lax.axis_size("dp")
-    return (out, query_grad, key_grad, value_grad, frame_grad, kernel_grad)
+    results = jnp.stack([out, query_grad, key_grad, value_grad, frame_grad])
+    spread = lax.all_to_all(
+        results.reshape(5, sub_count, rows, 1, group), "sb", 1, 3, tiled=True
+    ).reshape(5, rows, channels)
+    return (spread[0], spread[1], spread[2], spread[3], spread[4], kernel_grad)
 
 
 def solution(mesh):
-    placed = (
-        P(("dp", "seq"), None),
-        P(("dp", "seq"), None),
-        P(("dp", "seq"), None),
-        P(("dp", "seq"), None),
-        P(("dp", "seq"), None),
-        P("dp"),
-        P(),
-    )
+    seq_count = mesh.shape["seq"]
+    split_mesh = Mesh(
+        mesh.devices.reshape(mesh.shape["dp"], seq_count // GROUPS, GROUPS),
+        ("dp", "sa", "sb"),
+    )
+    rows_spec = P(("dp", "sa", "sb"), None)
+    placed = (rows_spec, rows_spec, rows_spec, rows_spec, rows_spec, P("dp"), P())
     return jax.shard_map(
         per_device,
-        mesh=mesh,
+        mesh=split_mesh,
         in_specs=placed,
-        out_specs=(
-            P(("dp", "seq"), None),
-            P(("dp", "seq"), None),
-            P(("dp", "seq"), None),
-            P(("dp", "seq"), None),
-            P(("dp", "seq"), None),
-            P(),
-        ),
+        out_specs=(rows_spec, rows_spec, rows_spec, rows_spec, rows_spec, P()),
         check_vma=False,
     )

time: 775 us -> 395 us (0.51)
  waiting for transfers between devices: 517 us -> 134 us
  local copies, waits for them, and re-layouts: 108 us -> 59.1 us
  starting transfers between devices: 4.41 us -> 34.3 us
  blocking collectives: 0 us -> 24 us
  other arithmetic: 64.8 us -> 52.1 us
    psum x1 -> x0, waiting for transfers between devices: 173 us -> none  [per_device(): kernel_total = lax.psum(kernel_part, ('dp', 'seq'))]
    all_gather x2 -> x1, waiting for transfers between devices: 175 us -> 46.7 us  [per_device(): lax.all_gather(jnp.concatenate([mixed[1], mixed[2]], axis=1), 'sa', axis=...]
    reduce_scatter x1, waiting for transfers between devices: 169 us -> 46.6 us  [per_device(): lax.psum_scatter(grad_terms.reshape(span, 2 * group).astype(jnp.bfloat16)...]
    ppermute x0 -> x8, waiting for transfers between devices: none -> 36.3 us  [butterfly_sum(): x = x + lax.ppermute(x, axis, [(i, i ^ step) for i in range(count)])]
    another operation x33 -> x1, local copies, waits for them, and re-layouts: 24.3 us -> 0.1 us  [per_device(): jnp.stack([jnp.sum(conv_float * extended[KERNEL - 1 - tap_index:KERNEL -...]
    all_to_all x0 -> x1, blocking collectives: none -> 24 us  [per_device(): lax.all_to_all(stacked.reshape(5, rows, sub_count, group), 'sb', 2, 1, ti...]
    ppermute x0 -> x8, starting transfers between devices: none -> 22.3 us  [butterfly_sum(): x = x + lax.ppermute(x, axis, [(i, i ^ step) for i in range(count)])]
    dynamic_update_slice x0 -> x9, local copies, waits for them, and re-layouts: none -> 15.9 us  [the longest x8 15.5 us: per_device(): lax.scan(gradient_block, jnp.zeros((row_count, head_count, HEAD_DIM), jnp...]
  transfers between devices with their start and end apart: 6 -> 13, of which waited for: 4 -> 11; matrix products, arithmetic and copies ran while one was open for 17% -> 2% of each run, Pallas kernels for 0% -> 0%
where the time goes in v1:
time: 395 us; the launch traced here: 390 us
  waiting for transfers between devices  134 us (34%)
  matrix products  71.1 us (18%)
  local copies, waits for them, and re-layouts  59.1 us (15%)
  other arithmetic  52.1 us (13%)
  starting transfers between devices  34.3 us (9%)
  blocking collectives  24 us (6%)
  between operations  15.7 us (4%)
    all_gather x1, waiting for transfers between devices, per_device(): lax.all_gather(jnp.concatenate([mixed[1], mixed[2]], axis=1), 'sa', axis=...  46.7 us
    reduce_scatter x1, waiting for transfers between devices, per_device(): lax.psum_scatter(grad_terms.reshape(span, 2 * group).astype(jnp.bfloat16)...  46.6 us
    ppermute x8, waiting for transfers between devices, butterfly_sum(): x = x + lax.ppermute(x, axis, [(i, i ^ step) for i in range(count)])  36.3 us
    all_to_all x1, blocking collectives, per_device(): lax.all_to_all(stacked.reshape(5, rows, sub_count, group), 'sb', 2, 1, ti...  24 us
    dot_general x8, matrix products, block_scores(): jnp.einsum('thd,khd->htk', query_heads, key_part, preferred_element_type=...  23.7 us
    ppermute x8, starting transfers between devices, butterfly_sum(): x = x + lax.ppermute(x, axis, [(i, i ^ step) for i in range(count)])  22.3 us
    lt x12, other arithmetic, block_scores(): block_start + jnp.arange(key_part.shape[0], dtype=jnp.int32) < length  15.6 us
    dynamic_slice x12, local copies, waits for them, and re-layouts, per_device(): lax.scan(running_total, start_state, (key_blocks, block_starts))  15.6 us
  transfers between devices with their start and end apart: 13, of which 11 were waited for; matrix products, arithmetic and copies ran while one was open for 2% of the time, Pallas kernels for 0%

profile of v1, /device:TPU:1, one launch (start us, length us, event | category | flops | bytes accessed | tf_op | source)
XLA Modules:
  0.0 390.4 jit_solution(232273346341479808)
XLA Ops:
  12.7 24.0 %all_to_all.30 = bf16[5,160,4,192]{3,1,0,2:T(8,128)(2,1)S(1)} all-to-all(bf16[5,160,4,192]{3,1,0,2:T(8,128)(2,1)S(1)} %copy.80), channel_id=1, replica_groups=mesh['dp'=16,'sa'=4,'sb'=4] {'sb'}, dimensions={2} | all-to-all | bytes 2457600 | tf_op jit(solution)/shard_map/all_to_all | solution.py:44
  41.2 46.7 %all-gather.2.cloned.1.call-done = bf16[2560,384]{1,0:T(8,128)(2,1)} async-done(((bf16[640,384]{1,0:T(8,128)(2,1)}), bf16[2560,384]{1,0:T(8,128)(2,1)}) %all-gather.2.cloned.1.call-update) | async-done | bytes 1966096 | tf_op jit(solution)/shard_map/all_gather | solution.py:50
  87.8 2.3 fusion.111
  91.5 1.9 reshape.121
  94.5 40.8 %while.37 = (s32[]{:T(128)}, f32[3,640]{1,0:T(4,128)S(1)}, f32[3,640]{1,0:T(4,128)S(1)}, s32[4]{0:T(128)}, s32[]{:T(128)}, /*index=5*/bf16[4,640,3,64]{1,3,2,0:T...) while((s32[]{:T(128)}, f32[3,640]{1,0:T(4,128)S(1)}, f32[3,640]{1,0:T(4,128)S(1)}, ...), condition=%wide.region_3.4_spmd.clone, body=%wide.region_0.3_spmd.clone.sunk | while | flops 165898880 | bytes 10424316 | solution.py:85
  97.1 4.1 %bitcast_reduce_fusion.2 = (f32[3,640]{1,0:T(4,128)S(1)}, f32[3,640,640]{2,1,0:T(8,128)}) fusion(pred[640]{0:T(1024)(128)(4,1)S(1)} %add_compare_fusion.7, bf16[640,3,64]{0,2,1:T(8,128)(2,1)S(1)} %get-tuple-element.670, bf16[4,640,3,64]{1,3,2,0:T(8,128)(2,1)} %get-tuple-element.669, s32[]{:T(128)} %get-tuple-element.655), kind=kOutput, calls=%fused_computation.1.clone.1 | convolution fusion | flops 160970880 | bytes 5415552 | tf_op jit(solution)/shard_map/while/body/eval_jaxpr/thd,khd->htk/dot_general | solution.py:65
  101.2 3.4 fusion.146
  107.3 4.1 %bitcast_reduce_fusion.2 = (f32[3,640]{1,0:T(4,128)S(1)}, f32[3,640,640]{2,1,0:T(8,128)}) fusion(pred[640]{0:T(1024)(128)(4,1)S(1)} %add_compare_fusion.7, bf16[640,3,64]{0,2,1:T(8,128)(2,1)S(1)} %get-tuple-element.670, bf16[4,640,3,64]{1,3,2,0:T(8,128)(2,1)} %get-tuple-element.669, s32[]{:T(128)} %get-tuple-element.655), kind=kOutput, calls=%fused_computation.1.clone.1 | convolution fusion | flops 160970880 | bytes 5415552 | tf_op jit(solution)/shard_map/while/body/eval_jaxpr/thd,khd->htk/dot_general | solution.py:65
  111.5 3.4 fusion.146
  117.5 4.1 %bitcast_reduce_fusion.2 = (f32[3,640]{1,0:T(4,128)S(1)}, f32[3,640,640]{2,1,0:T(8,128)}) fusion(pred[640]{0:T(1024)(128)(4,1)S(1)} %add_compare_fusion.7, bf16[640,3,64]{0,2,1:T(8,128)(2,1)S(1)} %get-tuple-element.670, bf16[4,640,3,64]{1,3,2,0:T(8,128)(2,1)} %get-tuple-element.669, s32[]{:T(128)} %get-tuple-element.655), kind=kOutput, calls=%fused_computation.1.clone.1 | convolution fusion | flops 160970880 | bytes 5415552 | tf_op jit(solution)/shard_map/while/body/eval_jaxpr/thd,khd->htk/dot_general | solution.py:65
  121.7 3.4 fusion.146
  127.7 4.1 %bitcast_reduce_fusion.2 = (f32[3,640]{1,0:T(4,128)S(1)}, f32[3,640,640]{2,1,0:T(8,128)}) fusion(pred[640]{0:T(1024)(128)(4,1)S(1)} %add_compare_fusion.7, bf16[640,3,64]{0,2,1:T(8,128)(2,1)S(1)} %get-tuple-element.670, bf16[4,640,3,64]{1,3,2,0:T(8,128)(2,1)} %get-tuple-element.669, s32[]{:T(128)} %get-tuple-element.655), kind=kOutput, calls=%fused_computation.1.clone.1 | convolution fusion | flops 160970880 | bytes 5415552 | tf_op jit(solution)/shard_map/while/body/eval_jaxpr/thd,khd->htk/dot_general | solution.py:65
  131.9 3.4 fusion.146
  137.0 24.5 %while.38 = (s32[]{:T(128)}, f32[640,3,64]{0,2,1:T(8,128)}, bf16[4,640,3,64]{1,3,2,0:T(8,128)(2,1)S(1)}, s32[4]{0:T(128)}, s32[]{:T(128)}, /*index=5*/bf16[4,640...) while((s32[]{:T(128)}, f32[640,3,64]{0,2,1:T(8,128)}, ...), condition=%wide.region_5.6_spmd.clone, body=%wide.region_4.5_spmd.clone.sunk | while | flops 319735040 | bytes 1733379 | solution.py:101
  139.5 3.4 fusion.151
  145.5 3.6 fusion.151
  151.6 3.6 fusion.151
  157.8 3.6 fusion.151
  164.0 7.1 %collective-permute-start = (bf16[31,192]{1,0:T(8,128)(2,1)S(1)}, bf16[31,192]{1,0:T(8,128)(2,1)S(1)}, u32[]{:S(2)}, u32[]{:S(2)}) collective-permute-start(bf16[31,192]{1,0:T(8,128)(2,1)S(1)} %slice.531), channel_id=1, source_target_pairs={{0,4},{4,8},{8,12},{1,5},{5,9},{9,13},{2,6},{6,10},{10,14},{3,7},{... | collective-permute-start | bytes 35720 | tf_op jit(solution)/shard_map/ppermute | solution.py:15
  172.4 7.1 %fusion.71 = (f32[192]{0:T(256)}, f32[192]{0:T(256)}, f32[192]{0:T(256)}, f32[192]{0:T(256)}, f32[192]{0:T(256)}, /*index=5*/f32[192]{0:T(256)}, f32[192]{0:T(25...) fusion(f32[671,192]{1,0:T(8,128)S(1)} %maximum_convert_fusion, ...), kind=kLoop, calls=%fused_computation.113 | loop fusion | flops 13636224 | bytes 16750720 | tf_op jit(solution)/shard_map/reduce_sum | solution.py:129
  180.8 4.1 %collective-permute-done.1 = bf16[31,192]{1,0:T(8,128)(2,1)S(1)} collective-permute-done((bf16[31,192]{1,0:T(8,128)(2,1)S(1)}, bf16[31,192]{1,0:T(8,128)(2,1)S(1)}, u32[]{:S(2)}, u32[]{:S(2)}) %collective-permute-start.1) | collective-permute-done | bytes 11936 | tf_op jit(solution)/shard_map/ppermute | solution.py:15
  185.0 3.1 fusion.75
  190.0 70.0 %while.39 = (s32[]{:T(128)}, f32[640,3,64]{0,2,1:T(8,128)}, bf16[4,640,384]{2,1,0:T(8,128)(2,1)}, bf16[4,640,3,64]{1,3,2,0:T(8,128)(2,1)}, s32[4]{0:T(128)}, /*i...) while((s32[]{:T(128)}, f32[640,3,64]{0,2,1:T(8,128)}, ...), condition=%wide.region_8.9_spmd.clone, body=%wide.region_7.8_spmd.clone.sunk | while | flops 800195840 | bytes 28292124 | solution.py:174
  190.0 1.8 fusion.162
  194.5 2.7 multiply_convert_fusion.3
  198.1 2.3 fusion.164
  201.2 2.0 copy.135
  203.2 1.8 constant_dynamic-update-slice_fusion.12
  205.1 2.3 fusion.163
  207.3 1.8 fusion.162
  211.8 2.7 multiply_convert_fusion.3
  215.4 2.3 fusion.164
  218.5 2.0 copy.135
  220.5 1.9 constant_dynamic-update-slice_fusion.12
  222.4 2.5 fusion.163
  224.9 1.8 fusion.162
  229.4 2.7 multiply_convert_fusion.3
  233.0 2.3 fusion.164
  236.1 2.0 copy.135
  238.1 1.9 constant_dynamic-update-slice_fusion.12
  240.0 2.5 fusion.163
  242.4 1.8 fusion.162
  246.9 2.7 multiply_convert_fusion.3
  250.5 2.3 fusion.164
  253.6 2.0 copy.135
  255.6 1.9 constant_dynamic-update-slice_fusion.12
  257.5 2.5 fusion.163
  260.0 2.9 fusion.70
  263.6 46.6 %reduce-scatter.2.cloned.1.call-done = bf16[640,384]{1,0:T(8,128)(2,1)} async-done(((bf16[2560,384]{1,0:T(8,128)(2,1)}), bf16[640,384]{1,0:T(8,128)(2,1)}) %reduce-scatter.2.cloned.1.call-update) | async-done | bytes 491536 | tf_op jit(solution)/shard_map/reduce_scatter | solution.py:179
  313.0 3.6 all-to-all-start.1
  317.3 1.9 collective-permute-start.2
  319.2 18.9 %collective-permute-done.2 = f32[32,768]{1,0:T(8,128)S(1)} collective-permute-done((f32[32,768]{1,0:T(8,128)S(1)}, f32[32,768]{1,0:T(8,128)S(1)}, u32[]{:S(2)}, u32[]{:S(2)}) %collective-permute-start.2) | collective-permute-done | bytes 98336 | tf_op jit(solution)/shard_map/ppermute | solution.py:23
  338.6 2.1 collective-permute-start.3
  340.8 2.0 collective-permute-done.3
  342.8 2.4 collective-permute-start.4
  345.2 2.1 collective-permute-done.4
  347.3 2.1 collective-permute-start.5
  349.4 5.4 %collective-permute-done.5 = f32[32,768]{1,0:T(8,128)S(1)} collective-permute-done((f32[32,768]{1,0:T(8,128)S(1)}, f32[32,768]{1,0:T(8,128)S(1)}, u32[]{:S(2)}, u32[]{:S(2)}) %collective-permute-start.5) | collective-permute-done | bytes 98336 | tf_op jit(solution)/shard_map/ppermute | solution.py:23
  354.8 6.6 %collective-permute-start.6 = (f32[32,768]{1,0:T(8,128)S(1)}, f32[32,768]{1,0:T(8,128)S(1)}, u32[]{:S(2)}, u32[]{:S(2)}) collective-permute-start(f32[32,768]{1,0:T(8,128)S(1)} %add.367), channel_id=1, source_target_pairs={{0,16},{16,0},{32,48},{48,32},{64,80},{80,64},{96,112},{112,96},{1... | collective-permute-start | bytes 294920 | tf_op jit(solution)/shard_map/ppermute | solution.py:23
  362.3 2.9 collective-permute-start.7
  365.3 2.7 collective-permute-done.7
  369.4 2.2 collective-permute-done.8
  371.5 2.9 collective-permute-start.9
  374.4 2.2 collective-permute-done.9
  (220 shorter events, 72.0 us)
Async XLA Ops:
  7.2 4.1 %copy-start.8 = (bf16[160,768]{1,0:T(8,128)(2,1)S(1)}, bf16[160,768]{1,0:T(8,128)(2,1)}, u32[]{:S(2)}) copy-start(bf16[160,768]{1,0:T(8,128)(2,1)} %param.16) | copy-start | bytes 737284
  7.2 4.4 %copy-start.9 = (bf16[160,768]{1,0:T(8,128)(2,1)S(1)}, bf16[160,768]{1,0:T(8,128)(2,1)}, u32[]{:S(2)}) copy-start(bf16[160,768]{1,0:T(8,128)(2,1)} %param.17) | copy-start | bytes 737284
  7.2 80.6 %all-gather.2.cloned.1.call-start = ((), (), s32[]{:S(2)}) async-start(), calls=%async_computation.3 | async-start | bytes 2457600 | tf_op jit(solution)/shard_map/all_gather | solution.py:50
  36.8 127.1 %copy-start.3 = (bf16[1,4,160,1,192]{4,2,0,1,3:T(8,128)(2,1)}, bf16[1,4,160,1,192]{4,2,0,1,3:T(8,128)(2,1)S(1)}, u32[]{:S(2)}) copy-start(bf16[1,4,160,1,192]{4,2,0,1,3:T(8,128)(2,1)S(1)} %get-tuple-element.447) | copy-start | bytes 737284
  37.8 272.4 %reduce-scatter.2.cloned.1.call-start = ((), (), s32[]{:S(2)}) async-start(), calls=%async_computation.4 | async-start | bytes 2457600 | tf_op jit(solution)/shard_map/reduce_scatter | solution.py:179
  40.0 1.2 copy-start.10
  161.4 1.0 copy-start.7
  162.4 9.9 %copy-start.11 = (f32[1,192]{1,0:T(1,128)S(1)}, f32[1,192]{1,0:T(1,128)}, u32[]{:S(2)}) copy-start(f32[1,192]{1,0:T(1,128)} %get-tuple-element.451) | copy-start | bytes 2308
  162.4 9.9 %copy-start.12 = (f32[1,192]{1,0:T(1,128)S(1)}, f32[1,192]{1,0:T(1,128)}, u32[]{:S(2)}) copy-start(f32[1,192]{1,0:T(1,128)} %get-tuple-element.452) | copy-start | bytes 2308
  162.4 9.9 %copy-start.13 = (f32[1,192]{1,0:T(1,128)S(1)}, f32[1,192]{1,0:T(1,128)}, u32[]{:S(2)}) copy-start(f32[1,192]{1,0:T(1,128)} %get-tuple-element.453) | copy-start | bytes 2308
  162.4 9.9 %copy-start.14 = (f32[1,192]{1,0:T(1,128)S(1)}, f32[1,192]{1,0:T(1,128)}, u32[]{:S(2)}) copy-start(f32[1,192]{1,0:T(1,128)} %get-tuple-element.454) | copy-start | bytes 2308
  162.4 9.9 %copy-start.15 = (f32[1,192]{1,0:T(1,128)S(1)}, f32[1,192]{1,0:T(1,128)}, u32[]{:S(2)}) copy-start(f32[1,192]{1,0:T(1,128)} %get-tuple-element.455) | copy-start | bytes 2308
  162.4 9.9 %copy-start.16 = (f32[1,192]{1,0:T(1,128)S(1)}, f32[1,192]{1,0:T(1,128)}, u32[]{:S(2)}) copy-start(f32[1,192]{1,0:T(1,128)} %get-tuple-element.456) | copy-start | bytes 2308
  162.4 9.9 %copy-start.17 = (f32[1,192]{1,0:T(1,128)S(1)}, f32[1,192]{1,0:T(1,128)}, u32[]{:S(2)}) copy-start(f32[1,192]{1,0:T(1,128)} %get-tuple-element.457) | copy-start | bytes 2308
  162.4 9.9 %copy-start.18 = (f32[1,192]{1,0:T(1,128)S(1)}, f32[1,192]{1,0:T(1,128)}, u32[]{:S(2)}) copy-start(f32[1,192]{1,0:T(1,128)} %get-tuple-element.458) | copy-start | bytes 2308
  162.4 9.9 %copy-start.19 = (f32[1,192]{1,0:T(1,128)S(1)}, f32[1,192]{1,0:T(1,128)}, u32[]{:S(2)}) copy-start(f32[1,192]{1,0:T(1,128)} %get-tuple-element.459) | copy-start | bytes 2308
  162.5 9.9 %copy-start.20 = (f32[1,192]{1,0:T(1,128)S(1)}, f32[1,192]{1,0:T(1,128)}, u32[]{:S(2)}) copy-start(f32[1,192]{1,0:T(1,128)} %get-tuple-element.460) | copy-start | bytes 2308
  162.5 9.9 %copy-start.21 = (f32[1,192]{1,0:T(1,128)S(1)}, f32[1,192]{1,0:T(1,128)}, u32[]{:S(2)}) copy-start(f32[1,192]{1,0:T(1,128)} %get-tuple-element.461) | copy-start | bytes 2308
  162.5 9.9 %copy-start.22 = (f32[1,192]{1,0:T(1,128)S(1)}, f32[1,192]{1,0:T(1,128)}, u32[]{:S(2)}) copy-start(f32[1,192]{1,0:T(1,128)} %get-tuple-element.462) | copy-start | bytes 2308
  162.5 9.9 %copy-start.23 = (f32[1,192]{1,0:T(1,128)S(1)}, f32[1,192]{1,0:T(1,128)}, u32[]{:S(2)}) copy-start(f32[1,192]{1,0:T(1,128)} %get-tuple-element.463) | copy-start | bytes 2308
  162.5 9.9 %copy-start.24 = (f32[1,192]{1,0:T(1,128)S(1)}, f32[1,192]{1,0:T(1,128)}, u32[]{:S(2)}) copy-start(f32[1,192]{1,0:T(1,128)} %get-tuple-element.464) | copy-start | bytes 2308
  162.5 9.9 %copy-start.25 = (f32[1,192]{1,0:T(1,128)S(1)}, f32[1,192]{1,0:T(1,128)}, u32[]{:S(2)}) copy-start(f32[1,192]{1,0:T(1,128)} %get-tuple-element.465) | copy-start | bytes 2308
  162.5 9.9 %copy-start.26 = (f32[1,192]{1,0:T(1,128)S(1)}, f32[1,192]{1,0:T(1,128)}, u32[]{:S(2)}) copy-start(f32[1,192]{1,0:T(1,128)} %get-tuple-element.466) | copy-start | bytes 2308
  162.5 9.9 %copy-start.27 = (f32[1,192]{1,0:T(1,128)S(1)}, f32[1,192]{1,0:T(1,128)}, u32[]{:S(2)}) copy-start(f32[1,192]{1,0:T(1,128)} %get-tuple-element.467) | copy-start | bytes 2308
  162.5 9.9 %copy-start.28 = (f32[1,192]{1,0:T(1,128)S(1)}, f32[1,192]{1,0:T(1,128)}, u32[]{:S(2)}) copy-start(f32[1,192]{1,0:T(1,128)} %get-tuple-element.468) | copy-start | bytes 2308
  163.8 8.3 %copy-start.1 = (f32[640,192]{1,0:T(8,128)}, f32[640,192]{1,0:T(8,128)S(1)}, u32[]{:S(2)}) copy-start(f32[640,192]{1,0:T(8,128)S(1)} %copy.87) | copy-start | bytes 1474564
  164.0 8.1 %collective-permute-start = (bf16[31,192]{1,0:T(8,128)(2,1)S(1)}, bf16[31,192]{1,0:T(8,128)(2,1)S(1)}, u32[]{:S(2)}, u32[]{:S(2)}) collective-permute-start(bf16[31,192]{1,0:T(8,128)(2,1)S(1)} %slice.531), channel_id=1, source_target_pairs={{0,4},{4,8},{8,12},{1,5},{5,9},{9,13},{2,6},{6,10},{10,14},{3,7},{... | collective-permute-start | bytes 35720 | tf_op jit(solution)/shard_map/ppermute | solution.py:15
  179.5 8.6 %copy-start.2 = (bf16[640,192]{1,0:T(8,128)(2,1)}, bf16[640,192]{1,0:T(8,128)(2,1)S(1)}, u32[]{:S(2)}) copy-start(bf16[640,192]{1,0:T(8,128)(2,1)S(1)} %get-tuple-element.432) | copy-start | bytes 737284
  179.5 5.4 %collective-permute-start.1 = (bf16[31,192]{1,0:T(8,128)(2,1)S(1)}, bf16[31,192]{1,0:T(8,128)(2,1)S(1)}, u32[]{:S(2)}, u32[]{:S(2)}) collective-permute-start(bf16[31,192]{1,0:T(8,128)(2,1)S(1)} %slice.596), channel_id=1, source_target_pairs={{4,0},{8,4},{12,8},{5,1},{9,5},{13,9},{6,2},{10,6},{14,10},{7,3},{... | collective-permute-start | bytes 35720 | tf_op jit(solution)/shard_map/ppermute | solution.py:15
  185.0 4.0 %copy-start.6 = (f32[640,3,64]{0,2,1:T(8,128)S(1)}, f32[640,3,64]{0,2,1:T(8,128)}, u32[]{:S(2)}) copy-start(f32[640,3,64]{0,2,1:T(8,128)} %get-tuple-element.146) | copy-start | bytes 1474564
  188.1 1.9 copy-start.4
  260.0 2.9 copy-start
  263.0 48.5 %copy-start.5 = (bf16[640,192]{1,0:T(8,128)(2,1)S(1)}, bf16[640,192]{1,0:T(8,128)(2,1)}, u32[]{:S(2)}) copy-start(bf16[640,192]{1,0:T(8,128)(2,1)} %copy-done.4) | copy-start | bytes 737284
  312.8 3.7 copy-start.29
  312.8 3.7 copy-start.30
  312.8 3.8 copy-start.31
  312.8 3.8 copy-start.32
  312.8 3.8 copy-start.33
  312.9 3.8 copy-start.34
  312.9 3.8 copy-start.35
  312.9 3.8 copy-start.36
  312.9 3.8 copy-start.37
  312.9 3.8 copy-start.38
  312.9 3.8 copy-start.39
  312.9 3.8 copy-start.40
  312.9 3.8 copy-start.41
  312.9 3.8 copy-start.42
  312.9 3.8 copy-start.43
  313.0 3.8 copy-start.44
  313.0 3.8 copy-start.45
  313.0 3.8 copy-start.46
  313.0 64.2 %all-to-all-start.1 = ((bf16[5,4,160,1,192]{4,2,3,0,1:T(8,128)(2,1)}), bf16[5,4,160,1,192]{4,2,3,0,1:T(8,128)(2,1)S(1)}, u32[]{:S(2)}, u32[]{:S(2)}) async-start(bf16[5,4,160,1,192]{4,2,3,0,1:T(8,128)(2,1)} %copy.93), calls=%async_computation.2 | async-start | bytes 3276800 | tf_op jit(solution)/shard_map/all_to_all | solution.py:194
  317.3 20.8 %collective-permute-start.2 = (f32[32,768]{1,0:T(8,128)S(1)}, f32[32,768]{1,0:T(8,128)S(1)}, u32[]{:S(2)}, u32[]{:S(2)}) collective-permute-start(f32[32,768]{1,0:T(8,128)S(1)} %dynamic_update_slice.9), channel_id=1, source_target_pairs={{0,1},{1,0},{2,3},{3,2},{4,5},{5,4},{6,7},{7,6},{8,9},{9,8},{10,11... | collective-permute-start | bytes 294920 | tf_op jit(solution)/shard_map/ppermute | solution.py:23
  338.6 4.1 %collective-permute-start.3 = (f32[32,768]{1,0:T(8,128)S(1)}, f32[32,768]{1,0:T(8,128)S(1)}, u32[]{:S(2)}, u32[]{:S(2)}) collective-permute-start(f32[32,768]{1,0:T(8,128)S(1)} %add.364), channel_id=1, source_target_pairs={{0,2},{1,3},{2,0},{3,1},{4,6},{5,7},{6,4},{7,5},{8,10},{9,11},{10,... | collective-permute-start | bytes 294920 | tf_op jit(solution)/shard_map/ppermute | solution.py:23
  342.8 4.5 %collective-permute-start.4 = (f32[32,768]{1,0:T(8,128)S(1)}, f32[32,768]{1,0:T(8,128)S(1)}, u32[]{:S(2)}, u32[]{:S(2)}) collective-permute-start(f32[32,768]{1,0:T(8,128)S(1)} %add.365), channel_id=1, source_target_pairs={{0,4},{4,0},{8,12},{12,8},{1,5},{5,1},{9,13},{13,9},{2,6},{6,2},{1... | collective-permute-start | bytes 294920 | tf_op jit(solution)/shard_map/ppermute | solution.py:23
  347.3 7.5 %collective-permute-start.5 = (f32[32,768]{1,0:T(8,128)S(1)}, f32[32,768]{1,0:T(8,128)S(1)}, u32[]{:S(2)}, u32[]{:S(2)}) collective-permute-start(f32[32,768]{1,0:T(8,128)S(1)} %add.366), channel_id=1, source_target_pairs={{0,8},{4,12},{8,0},{12,4},{1,9},{5,13},{9,1},{13,5},{2,10},{6,14},... | collective-permute-start | bytes 294920 | tf_op jit(solution)/shard_map/ppermute | solution.py:23
  354.8 7.5 %collective-permute-start.6 = (f32[32,768]{1,0:T(8,128)S(1)}, f32[32,768]{1,0:T(8,128)S(1)}, u32[]{:S(2)}, u32[]{:S(2)}) collective-permute-start(f32[32,768]{1,0:T(8,128)S(1)} %add.367), channel_id=1, source_target_pairs={{0,16},{16,0},{32,48},{48,32},{64,80},{80,64},{96,112},{112,96},{1... | collective-permute-start | bytes 294920 | tf_op jit(solution)/shard_map/ppermute | solution.py:23
  362.3 5.6 %collective-permute-start.7 = (f32[32,768]{1,0:T(8,128)S(1)}, f32[32,768]{1,0:T(8,128)S(1)}, u32[]{:S(2)}, u32[]{:S(2)}) collective-permute-start(f32[32,768]{1,0:T(8,128)S(1)} %add.368), channel_id=1, source_target_pairs={{0,32},{16,48},{32,0},{48,16},{64,96},{80,112},{96,64},{112,80},{1... | collective-permute-start | bytes 294920 | tf_op jit(solution)/shard_map/ppermute | solution.py:23
  367.9 3.6 collective-permute-start.8
  371.5 5.1 %collective-permute-start.9 = (f32[32,768]{1,0:T(8,128)S(1)}, f32[32,768]{1,0:T(8,128)S(1)}, u32[]{:S(2)}, u32[]{:S(2)}) collective-permute-start(f32[32,768]{1,0:T(8,128)S(1)} %add.370), channel_id=1, source_target_pairs={{0,128},{16,144},{32,160},{48,176},{64,192},{80,208},{96,224},{112... | collective-permute-start | bytes 294920 | tf_op jit(solution)/shard_map/ppermute | solution.py:23
Sparse Core Ops, SparseCore 0:
  38.0 49.8 all-gather.1
  260.1 50.0 reduce-scatter.1
